TPU v7x, 128 devices: a whole 4x4x4 slice. The times are simulated.
128 devices in a mesh: blk: 32 (over y, x, core), grp: 4 (over z).
Axes of the slice: x: 4, y: 4, z: 4, core: 2. Of those that a mesh axis runs over, the one named last changes fastest.
Arguments:
- sky_map: bfloat16 [256, 1048576], P(None, ('blk', 'grp')), may hold values from -128 to 128
- fg_templates: bfloat16 [256, 16], replicated, may hold values from -0.375 to 0.375
- cycle_len: int32 [512], P(('blk', 'grp')), may hold values from 512 to 2048, as said below
- beam_profile: float32 [8, 1024], replicated, may hold values from 0.2 to 2
- beam_index: int32 [256], P('blk'), may hold values from 0 to 7
Outputs:
- filtered: float32 [1024, 256, 2, 1024], P(None, 'blk', None, 'grp')
Inputs may be any that keep to these rules, and one draw needn't show every extreme that they name: `cycle_len`: some cycle has exactly 2048 pixels.
All inputs are finite; a program needn't handle non-finite values.
Results may differ from a plain program's by a relative error of at most 0.0064.
Values may be sent and summed in bfloat16 or wider, within the bound.
No kernel may reach another device: no remote copies, remote signals or barrier semaphores. Data moves between devices by JAX's collectives and lax.ppermute only.
A program may use at most 192 MiB of HBM per device.

v0:
```python
import jax
import jax.numpy as jnp
from jax import lax
from jax.sharding import PartitionSpec as P

RPIX = 2048
L = 1024
M_DEV = 256


def cycle_table(length, m_width):
    slots = jnp.arange(RPIX, dtype=jnp.int32)
    orders = jnp.arange(m_width, dtype=jnp.int32)
    phase = orders[None, :] * (2 * slots[:, None] + 1) % (2 * length)
    angle = jnp.pi * phase.astype(jnp.float32) / length.astype(jnp.float32)
    weight = jnp.where(slots < length, 1.0, 0.0).astype(jnp.float32) * lax.rsqrt(
        length.astype(jnp.float32)
    )
    table = jnp.concatenate([jnp.cos(angle), -jnp.sin(angle)], axis=1) * weight[:, None]
    return table.astype(jnp.bfloat16)


def theta_table(cycle_ids, n_cycle):
    degrees = jnp.arange(L, dtype=jnp.int32)
    odd = 2 * cycle_ids + 1
    phase = degrees[:, None] * odd[None, :] % (4 * n_cycle)
    angle = jnp.pi * phase.astype(jnp.float32) / (2.0 * n_cycle)
    weight = jnp.sin(jnp.pi * odd.astype(jnp.float32) / (2.0 * n_cycle)) * (
        2.0 / jnp.sqrt(jnp.float32(n_cycle))
    )
    return (jnp.cos(angle) * weight[None, :]).astype(jnp.bfloat16)


def body(sky_map, fg_templates, cycle_len, beam_profile, beam_index):
    n_blk = lax.axis_size("blk")
    n_grp = lax.axis_size("grp")
    cycle_dev = cycle_len.shape[0]
    n_chan = sky_map.shape[0]
    chan_dev = n_chan // n_blk
    m_width = M_DEV * n_grp
    n_cycle = cycle_dev * n_blk * n_grp
    slots = jnp.arange(RPIX, dtype=jnp.int32)
    valid = (slots[None, :] < cycle_len[:, None]).reshape(-1)
    masked = jnp.where(valid[None, :], sky_map, jnp.zeros((), jnp.bfloat16))
    mode_amps = jnp.dot(fg_templates.T, masked, preferred_element_type=jnp.float32).astype(
        jnp.bfloat16
    )
    gram_part = jnp.dot(mode_amps, mode_amps.T, preferred_element_type=jnp.float32)
    cross_part = lax.dot_general(
        mode_amps, masked, (((1,), (1,)), ((), ())), preferred_element_type=jnp.float32
    )
    amps_wide = mode_amps.astype(jnp.float32)
    gram_sum = lax.psum(gram_part, ("blk", "grp"))
    lower = jnp.linalg.cholesky(gram_sum)
    basis = jax.scipy.linalg.solve_triangular(lower, amps_wide, lower=True)
    proj_part = jax.scipy.linalg.solve_triangular(lower, cross_part, lower=True)
    projected = lax.psum(proj_part, ("blk", "grp"))
    correction = jnp.dot(projected.T, basis, precision=lax.Precision.HIGHEST)
    cleaned = (masked.astype(jnp.float32) - correction).astype(jnp.bfloat16)
    pieces = []
    for local in range(cycle_dev):
        block = cleaned[:, local * RPIX : (local + 1) * RPIX]
        table = cycle_table(cycle_len[local], m_width)
        pieces.append(
            jnp.dot(block, table, preferred_element_type=jnp.float32).astype(jnp.bfloat16)
        )
    fourier = jnp.stack(pieces, 0).reshape(cycle_dev, n_chan, 2, m_width)
    position = jnp.arange(n_cycle, dtype=jnp.int32)
    moved = lax.all_to_all(
        lax.all_to_all(fourier, "blk", split_axis=1, concat_axis=0, tiled=True),
        "grp",
        split_axis=3,
        concat_axis=0,
        tiled=True,
    )
    group_id = position // (n_blk * cycle_dev)
    block_id = position // cycle_dev % n_blk
    cycle_ids = (block_id * n_grp + group_id) * cycle_dev + position % cycle_dev
    moved = moved.reshape(n_cycle, chan_dev * 2 * M_DEV)
    theta_tab = theta_table(cycle_ids, n_cycle)
    harmonic = jnp.dot(theta_tab, moved, preferred_element_type=jnp.float32).reshape(
        L, chan_dev, 2, M_DEV
    )
    onehot = (
        beam_index[:, None] == jnp.arange(beam_profile.shape[0], dtype=jnp.int32)[None, :]
    ).astype(jnp.float32)
    profiles = jnp.dot(onehot, beam_profile, precision=lax.Precision.HIGHEST)
    shaped = harmonic * profiles.T[:, :, None, None]
    orders = lax.axis_index("grp") * M_DEV + jnp.arange(M_DEV, dtype=jnp.int32)
    mweight = 0.25 + orders.astype(jnp.float32) / m_width
    weighted = shaped * mweight[None, None, None, :]
    power_part = jnp.sum(weighted * weighted, axis=(0, 2, 3))
    power = lax.psum(power_part, "grp")
    return weighted * lax.rsqrt(power / (2.0 * L * m_width) + 1e-06)[None, :, None, None]


def solution(mesh):
    return jax.shard_map(
        body,
        mesh=mesh,
        in_specs=(P(None, ("blk", "grp")), P(), P(("blk", "grp")), P(), P("blk")),
        out_specs=P(None, "blk", None, "grp"),
        check_vma=False,
    )
```

profile of v0, /device:TPU:0, one launch (start us, length us, event | category | flops | bytes accessed | tf_op | source)
XLA Modules:
  0.0 859.5 jit_solution(13465190245039165098)
XLA Ops:
  0.0 0.0 copy-start
  0.0 1.4 fusion.120
  6.2 0.7 fusion.87
  7.0 2.9 convolution_convert_fusion
  9.9 0.2 fusion.121
  10.1 3.4 fusion.50
  13.5 68.2 %psum.21 = f32[16,16]{0,1:T(8,128)S(1)} all-reduce(f32[16,16]{0,1:T(8,128)S(1)} %fusion.121), channel_id=1, replica_groups=mesh['blk'=32,'grp'=4] {'blk','grp'}, use_global_device_ids=true, to_apply=%region_0.1 | all-reduce | flops 256 | bytes 2048 | tf_op jit(solution)/shard_map/psum | solution.py:53
  81.7 0.1 copy.38
  81.8 1.5 cholesky.16
  83.3 0.7 compare_reduce_fusion
  84.0 0.7 fusion.88
  84.7 1.2 custom-call.10
  85.9 0.4 fusion.89
  86.3 0.2 fusion.91
  86.5 62.3 %psum.22 = f32[16,256]{1,0:T(8,128)S(1)} all-reduce(f32[16,256]{1,0:T(8,128)S(1)} %fusion.91), channel_id=1, replica_groups=mesh['blk'=32,'grp'=4] {'blk','grp'}, use_global_device_ids=true, to_apply=%region_3.4 | all-reduce | flops 4096 | bytes 32768 | tf_op jit(solution)/shard_map/psum | solution.py:57
  148.9 0.7 select_multiply_fusion.3
  149.6 8.9 %fusion.5 = bf16[256,8192]{1,0:T(8,128)(2,1)S(1)} fusion(f32[16,256]{1,0:T(8,128)S(1)} %psum.22, f32[16,8192]{1,0:T(8,128)S(1)} %fusion.89, bf16[256,8192]{1,0:T(8,128)(2,1)} %param.5, pred[8192]{0:T(1024)(128)(4,1)S(1)} %bitcast.62), kind=kOutput, calls=%fused_computation.16 | convolution fusion | flops 411041792 | bytes 8937472 | tf_op jit(solution)/shard_map/dot_general | solution.py:58
  158.5 0.0 copy-start.1
  158.5 451.2 %fusion.49 = (f32[2048,1024]{1,0:T(8,128)S(1)}, f32[2048,1024]{1,0:T(8,128)}, f32[2048,1024]{1,0:T(8,128)}, f32[2048,1024]{1,0:T(8,128)}, f32[2048,1024]{1,0:T(8...) fusion(f32[]{:T(128)S(6)} %convert_element_type.91, pred[]{:T(512)S(6)} %lt.110, ...), kind=kLoop, calls=%fused_computation.64 | loop fusion | flops 94371840 | bytes 67117088 | tf_op jit(solution)/shard_map/cos | solution.py:19
  609.7 0.0 copy-done.1
  609.7 6.3 fusion.51
  616.0 0.8 stack.15
  616.8 0.6 select_multiply_fusion.2
  617.4 8.5 fusion.54
  626.0 0.8 stack.16
  626.8 0.6 select_multiply_fusion.1
  627.4 9.5 %fusion.57 = bf16[256,2048]{1,0:T(8,128)(2,1)} fusion(f32[2048,1024]{1,0:T(8,128)} %get-tuple-element.7, f32[2048,1024]{1,0:T(8,128)} %get-tuple-element.10, f32[2048]{0:T(1024)S(1)} %select_multiply_fusion.1, bf16[256,8192]{1,0:T(8,128)(2,1)} %copy-done.1), kind=kOutput, calls=%fused_computation.72 | convolution fusion | flops 2160590848 | bytes 18882560 | tf_op jit(solution)/shard_map/dot_general | solution.py:65
  636.9 1.8 stack.17
  638.7 0.6 select_multiply_fusion
  639.3 9.5 %fusion.60 = bf16[256,2048]{1,0:T(8,128)(2,1)} fusion(f32[2048,1024]{1,0:T(8,128)} %get-tuple-element.8, f32[2048,1024]{1,0:T(8,128)} %get-tuple-element.9, f32[2048]{0:T(1024)S(1)} %select_multiply_fusion, bf16[256,8192]{1,0:T(8,128)(2,1)} %copy-done.1), kind=kOutput, calls=%fused_computation.73 | convolution fusion | flops 2160590848 | bytes 18882560 | tf_op jit(solution)/shard_map/dot_general | solution.py:65
  648.8 2.6 stack.18
  651.4 7.6 pad_maximum_fusion
  659.0 55.9 %all_to_all.33 = bf16[4,256,2,1024]{3,2,0,1:T(2,128)(2,1)S(1)} all-to-all(bf16[4,256,2,1024]{3,2,0,1:T(2,128)(2,1)S(1)} %pad_maximum_fusion), channel_id=1, replica_groups=mesh['blk'=32,'grp'=4] {'blk'}, dimensions={1} | all-to-all | bytes 8388608 | tf_op jit(solution)/shard_map/all_to_all | solution.py:70
  714.9 2.3 copy.55
  717.3 2.5 copy.44
  719.7 7.3 copy.45
  727.0 4.9 all-to-all-start.1
  731.9 0.1 sine_multiply_fusion
  732.0 0.0 copy-done
  732.0 0.2 convolution_bitcast_fusion
  732.2 49.1 %all-to-all-done.1 = bf16[128,8,2,1024]{0,1,2,3:T(8,128)(2,1)} async-done(((bf16[128,8,2,1024]{0,1,2,3:T(8,128)(2,1)}), bf16[128,8,2,1024]{0,1,2,3:T(8,128)(2,1)}, u32[]{:S(2)}, u32[]{:S(2)}) %all-to-all-start.1) | async-done | bytes 4194336 | tf_op jit(solution)/shard_map/all_to_all | solution.py:69
  781.3 9.0 %copy.47 = bf16[4,128,8,2,256]{4,3,2,1,0:T(2,128)(2,1)} copy(bf16[4,128,8,2,256]{1,2,3,4,0:T(8,128)(2,1)} %bitcast.18) | data formatting | bytes 8388608 | tf_op jit(solution)/shard_map/all_to_all | solution.py:69
  790.3 7.8 reshape.135
  798.1 6.5 copy.48
  804.6 17.2 %multiply_reduce_fusion = (f32[8]{0:T(128)S(1)}, f32[1024,8,2,256]{3,0,2,1:T(8,128)}) fusion(f32[256]{0:T(256)S(1)} %multiply_add_fusion.1, f32[1024,8]{0,1:T(8,128)S(1)} %convolution_bitcast_fusion, bf16[8,2,256,512]{3,2,1,0:T(8,128)(2,1)} %bitcast.55, f32[512]{0:T(512)S(1)} %sine_multiply_fusion, s32[512]{0:T(512)S(1)} %fusion.104), kind=kOutput, calls=%fused_computation.8 | convolution fusion | flops 4320133120 | bytes 21009440 | tf_op jit(solution)/shard_map/dot_general | solution.py:81
  821.9 8.8 %psum.23 = f32[8]{0:T(128)S(1)} all-reduce(f32[8]{0:T(128)S(1)} %get-tuple-element.17), channel_id=1, replica_groups=mesh['blk'=32,'grp'=4] {'grp'}, use_global_device_ids=true, to_apply=%region_5.6 | all-reduce | flops 8 | bytes 64 | tf_op jit(solution)/shard_map/psum | solution.py:93
  830.7 7.0 fusion.4
  837.8 21.5 %copy.49 = f32[1024,8,2,256]{3,2,1,0:T(2,128)} copy(f32[1024,8,2,256]{3,0,2,1:T(8,128)S(1)} %fusion.4) | data formatting | bytes 33554432 | tf_op jit(solution)/shard_map/mul | solution.py:94
  (9 shorter events, 0.1 us)
Async XLA Ops:
  0.0 732.0 %copy-start = (f32[8,1024]{1,0:T(8,128)S(1)}, f32[8,1024]{1,0:T(8,128)}, u32[]{:S(2)}) copy-start(f32[8,1024]{1,0:T(8,128)} %param.8) | copy-start | bytes 98308
  158.5 451.2 %copy-start.1 = (bf16[256,8192]{1,0:T(8,128)(2,1)}, bf16[256,8192]{1,0:T(8,128)(2,1)S(1)}, u32[]{:S(2)}) copy-start(bf16[256,8192]{1,0:T(8,128)(2,1)S(1)} %fusion.5) | copy-start | bytes 12582916
  719.7 12.3 %copy-start.2 = (s32[8]{0:T(128)S(1)}, s32[8]{0:T(128)}, u32[]{:S(2)}) copy-start(s32[8]{0:T(128)} %param.9) | copy-start | bytes 100
  727.0 54.3 %all-to-all-start.1 = ((bf16[128,8,2,1024]{0,1,2,3:T(8,128)(2,1)}), bf16[128,8,2,1024]{0,1,2,3:T(8,128)(2,1)}, u32[]{:S(2)}, u32[]{:S(2)}) async-start(bf16[128,8,2,1024]{0,1,2,3:T(8,128)(2,1)} %copy.45), calls=%async_computation.1 | async-start | bytes 8388608 | tf_op jit(solution)/shard_map/all_to_all | solution.py:69
where the time goes:
time: 867 us; the launch traced here: 859 us
  other arithmetic  473 us (55%)
  blocking collectives  195 us (22%)
  matrix products  67.2 us (8%)
  local copies, waits for them, and re-layouts  64.4 us (7%)
  waiting for transfers between devices  49.1 us (6%)
    cos x1, other arithmetic, cycle_table(): jnp.cos(angle)  451 us
    psum x1, blocking collectives, body(): gram_sum = lax.psum(gram_part, ('blk', 'grp'))  68.2 us
    psum x1, blocking collectives, body(): projected = lax.psum(proj_part, ('blk', 'grp'))  62.3 us
    all_to_all x1, blocking collectives, body(): lax.all_to_all(fourier, 'blk', split_axis=1, concat_axis=0, tiled=True)  55.9 us
    all_to_all x1, waiting for transfers between devices, body(): lax.all_to_all(lax.all_to_all(fourier, 'blk', split_axis=1, concat_axis=0...  49.1 us
    dot_general x4, matrix products, body(): jnp.dot(block, table, preferred_element_type=jnp.float32)  33.9 us
    mul x1, local copies, waits for them, and re-layouts, body(): weighted * lax.rsqrt(power / (2.0 * L * m_width) + 1e-06)[None, :, None,...  21.5 us
  transfers between devices with their start and end apart: 1, of which 1 were waited for; matrix products, arithmetic and copies ran while one was open for 0% of the time, Pallas kernels for 0%

commit v1 on v0

--- a/solution.py
+++ b/solution.py
@@ -6,6 +6,13 @@
 RPIX = 2048
 L = 1024
 M_DEV = 256
+
+
+def stacked_exchange(block, name, split, join):
+    count = lax.axis_size(name)
+    blocks = jnp.stack(jnp.split(block, count, axis=split), axis=0)
+    blocks = lax.all_to_all(blocks, name, split_axis=0, concat_axis=0)
+    return jnp.concatenate(blocks, axis=join)
 
 
 def cycle_table(length, m_width):
@@ -66,12 +73,8 @@
         )
     fourier = jnp.stack(pieces, 0).reshape(cycle_dev, n_chan, 2, m_width)
     position = jnp.arange(n_cycle, dtype=jnp.int32)
-    moved = lax.all_to_all(
-        lax.all_to_all(fourier, "blk", split_axis=1, concat_axis=0, tiled=True),
-        "grp",
-        split_axis=3,
-        concat_axis=0,
-        tiled=True,
+    moved = stacked_exchange(
+        lax.all_to_all(fourier, "blk", split_axis=1, concat_axis=0, tiled=True), "grp", 3, 0
     )
     group_id = position // (n_blk * cycle_dev)
     block_id = position // cycle_dev % n_blk

time: 867 us -> 860 us (level)
  local copies, waits for them, and re-layouts: 64.4 us -> 55.1 us
    all_to_all x3 -> x2, local copies, waits for them, and re-layouts: 12.1 us -> 2.96 us  [body(): lax.all_to_all(fourier, 'blk', split_axis=1, concat_axis=0, tiled=True)]
where the time goes in v1:
time: 860 us; the launch traced here: 853 us
  other arithmetic  475 us (55%)
  blocking collectives  195 us (23%)
  matrix products  67.2 us (8%)
  local copies, waits for them, and re-layouts  55.1 us (6%)
  waiting for transfers between devices  49.1 us (6%)
    cos x1, other arithmetic, cycle_table(): jnp.cos(angle)  451 us
    psum x1, blocking collectives, body(): gram_sum = lax.psum(gram_part, ('blk', 'grp'))  68.2 us
    psum x1, blocking collectives, body(): projected = lax.psum(proj_part, ('blk', 'grp'))  62.3 us
    all_to_all x1, blocking collectives, body(): lax.all_to_all(fourier, 'blk', split_axis=1, concat_axis=0, tiled=True)  55.7 us
    all_to_all x1, waiting for transfers between devices, stacked_exchange(): blocks = lax.all_to_all(blocks, name, split_axis=0, concat_axis=0)  49.1 us
    dot_general x4, matrix products, body(): jnp.dot(block, table, preferred_element_type=jnp.float32)  33.9 us
    mul x1, local copies, waits for them, and re-layouts, body(): weighted * lax.rsqrt(power / (2.0 * L * m_width) + 1e-06)[None, :, None,...  21.5 us
    dot_general x1, matrix products, body(): jnp.dot(theta_tab, moved, preferred_element_type=jnp.float32)  17.2 us
  transfers between devices with their start and end apart: 1, of which 1 were waited for; matrix products, arithmetic and copies ran while one was open for 0% of the time, Pallas kernels for 0%

profile of v1, /device:TPU:0, one launch (start us, length us, event | category | flops | bytes accessed | tf_op | source)
XLA Modules:
  0.0 852.5 jit_solution(15851574456957401119)
XLA Ops:
  0.0 0.0 copy-start
  0.0 1.4 fusion.120
  6.2 0.7 fusion.87
  7.0 2.9 convolution_convert_fusion
  9.9 0.2 fusion.121
  10.1 3.4 fusion.50
  13.5 68.2 %psum.21 = f32[16,16]{0,1:T(8,128)S(1)} all-reduce(f32[16,16]{0,1:T(8,128)S(1)} %fusion.121), channel_id=1, replica_groups=mesh['blk'=32,'grp'=4] {'blk','grp'}, use_global_device_ids=true, to_apply=%region_0.1 | all-reduce | flops 256 | bytes 2048 | tf_op jit(solution)/shard_map/psum | solution.py:60
  81.7 0.1 copy.26
  81.8 1.5 cholesky.16
  83.3 0.7 compare_reduce_fusion
  84.0 0.7 fusion.88
  84.7 1.2 custom-call.10
  85.9 0.4 fusion.89
  86.4 0.2 fusion.91
  86.6 62.3 %psum.22 = f32[16,256]{1,0:T(8,128)S(1)} all-reduce(f32[16,256]{1,0:T(8,128)S(1)} %fusion.91), channel_id=1, replica_groups=mesh['blk'=32,'grp'=4] {'blk','grp'}, use_global_device_ids=true, to_apply=%region_3.4 | all-reduce | flops 4096 | bytes 32768 | tf_op jit(solution)/shard_map/psum | solution.py:64
  148.9 0.7 select_multiply_fusion.3
  149.7 8.9 %fusion.5 = bf16[256,8192]{1,0:T(8,128)(2,1)S(1)} fusion(f32[16,256]{1,0:T(8,128)S(1)} %psum.22, f32[16,8192]{1,0:T(8,128)S(1)} %fusion.89, bf16[256,8192]{1,0:T(8,128)(2,1)} %param.5, pred[8192]{0:T(1024)(128)(4,1)S(1)} %bitcast.67), kind=kOutput, calls=%fused_computation.16 | convolution fusion | flops 411041792 | bytes 8937472 | tf_op jit(solution)/shard_map/dot_general | solution.py:65
  158.5 451.2 %fusion.49 = (f32[2048,1024]{1,0:T(8,128)S(1)}, f32[2048,1024]{1,0:T(8,128)}, f32[2048,1024]{1,0:T(8,128)}, f32[2048,1024]{1,0:T(8,128)}, f32[2048,1024]{1,0:T(8...) fusion(f32[]{:T(128)S(6)} %convert_element_type.91, pred[]{:T(512)S(6)} %lt.110, ...), kind=kLoop, calls=%fused_computation.65 | loop fusion | flops 94371840 | bytes 67117088 | tf_op jit(solution)/shard_map/cos | solution.py:26
  609.7 0.0 copy-done.1
  609.7 6.3 fusion.51
  616.1 0.8 stack.30
  616.9 0.6 select_multiply_fusion.2
  617.4 8.5 fusion.54
  626.0 0.8 stack.31
  626.8 0.6 select_multiply_fusion.1
  627.4 9.5 %fusion.57 = bf16[256,2048]{1,0:T(8,128)(2,1)} fusion(f32[2048,1024]{1,0:T(8,128)} %get-tuple-element.11, f32[2048,1024]{1,0:T(8,128)} %get-tuple-element.14, f32[2048]{0:T(1024)S(1)} %select_multiply_fusion.1, bf16[256,8192]{1,0:T(8,128)(2,1)} %copy-done.1), kind=kOutput, calls=%fused_computation.73 | convolution fusion | flops 2160590848 | bytes 18882560 | tf_op jit(solution)/shard_map/dot_general | solution.py:72
  636.9 1.8 stack.32
  638.7 0.6 select_multiply_fusion
  639.3 9.5 %fusion.60 = bf16[256,2048]{1,0:T(8,128)(2,1)} fusion(f32[2048,1024]{1,0:T(8,128)} %get-tuple-element.12, f32[2048,1024]{1,0:T(8,128)} %get-tuple-element.13, f32[2048]{0:T(1024)S(1)} %select_multiply_fusion, bf16[256,8192]{1,0:T(8,128)(2,1)} %copy-done.1), kind=kOutput, calls=%fused_computation.74 | convolution fusion | flops 2160590848 | bytes 18882560 | tf_op jit(solution)/shard_map/dot_general | solution.py:72
  648.8 2.6 stack.33
  651.5 7.6 pad_maximum_fusion
  659.1 55.7 %all_to_all.23 = bf16[4,256,2,1024]{3,2,0,1:T(2,128)(2,1)S(1)} all-to-all(bf16[4,256,2,1024]{3,2,0,1:T(2,128)(2,1)S(1)} %pad_maximum_fusion), channel_id=1, replica_groups=mesh['blk'=32,'grp'=4] {'blk'}, dimensions={1} | all-to-all | bytes 8388608 | tf_op jit(solution)/shard_map/all_to_all | solution.py:77
  714.7 2.3 copy.40
  717.1 0.6 copy.32
  717.7 0.3 slice_bitcast_fusion.3
  718.1 0.0 copy-start.2
  718.1 2.3 pad_maximum_fusion.1
  720.4 5.1 all-to-all-start.1
  725.5 0.1 sine_multiply_fusion
  725.5 0.2 convolution_bitcast_fusion
  725.7 49.1 %all-to-all-done.1 = bf16[4,128,8,2,256]{4,2,3,1,0:T(8,128)(2,1)} async-done(((bf16[4,128,8,2,256]{4,2,3,1,0:T(8,128)(2,1)}), bf16[4,128,8,2,256]{4,2,3,1,0:T(8,128)(2,1)}, u32[]{:S(2)}, u32[]{:S(2)}) %all-to-all-start.1) | async-done | bytes 4194336 | tf_op jit(solution)/shard_map/all_to_all | solution.py:14
  774.8 8.5 copy.33
  783.4 7.8 reshape_reshape.3
  791.1 6.5 copy.34
  797.7 17.2 %multiply_reduce_fusion = (f32[8]{0:T(128)S(1)}, f32[1024,8,2,256]{3,0,2,1:T(8,128)}) fusion(f32[256]{0:T(256)S(1)} %multiply_add_fusion.1, f32[1024,8]{0,1:T(8,128)S(1)} %convolution_bitcast_fusion, bf16[8,2,256,512]{3,2,1,0:T(8,128)(2,1)} %bitcast.60, f32[512]{0:T(512)S(1)} %sine_multiply_fusion, s32[512]{0:T(512)S(1)} %fusion.104), kind=kOutput, calls=%fused_computation.8 | convolution fusion | flops 4320133120 | bytes 21009440 | tf_op jit(solution)/shard_map/dot_general | solution.py:84
  814.9 8.9 %psum.23 = f32[8]{0:T(128)S(1)} all-reduce(f32[8]{0:T(128)S(1)} %get-tuple-element.21), channel_id=1, replica_groups=mesh['blk'=32,'grp'=4] {'grp'}, use_global_device_ids=true, to_apply=%region_5.6 | all-reduce | flops 8 | bytes 64 | tf_op jit(solution)/shard_map/psum | solution.py:96
  823.8 7.0 fusion.4
  830.8 21.5 %copy.35 = f32[1024,8,2,256]{3,2,1,0:T(2,128)} copy(f32[1024,8,2,256]{3,0,2,1:T(8,128)S(1)} %fusion.4) | data formatting | bytes 33554432 | tf_op jit(solution)/shard_map/mul | solution.py:97
  (10 shorter events, 0.1 us)
Async XLA Ops:
  0.0 725.5 %copy-start = (f32[8,1024]{1,0:T(8,128)S(1)}, f32[8,1024]{1,0:T(8,128)}, u32[]{:S(2)}) copy-start(f32[8,1024]{1,0:T(8,128)} %param.8) | copy-start | bytes 98308
  158.5 451.2 %copy-start.1 = (bf16[256,8192]{1,0:T(8,128)(2,1)}, bf16[256,8192]{1,0:T(8,128)(2,1)S(1)}, u32[]{:S(2)}) copy-start(bf16[256,8192]{1,0:T(8,128)(2,1)S(1)} %fusion.5) | copy-start | bytes 12582916
  718.1 7.5 copy-start.2
  720.4 54.5 %all-to-all-start.1 = ((bf16[4,128,8,2,256]{4,2,3,1,0:T(8,128)(2,1)}), bf16[4,128,8,2,256]{4,2,3,1,0:T(8,128)(2,1)}, u32[]{:S(2)}, u32[]{:S(2)}) async-start(bf16[4,128,8,2,256]{4,2,3,1,0:T(8,128)(2,1)} %pad_maximum_fusion.1), calls=%async_computation.1 | async-start | bytes 8388608 | tf_op jit(solution)/shard_map/all_to_all | solution.py:14
